TPU v7x, 512 devices: a whole 4x8x8 slice. The times are simulated.
512 devices in a mesh: seq: 64 (over x, z_lo, y), tp: 8 (over z_hi, core).
Axes of the slice: x: 4, y: 8, z: 8 (z_hi: 4, z_lo: 2; z = z_hi * 2 + z_lo), core: 2. Of those that a mesh axis runs over, the one named last changes fastest.
Arguments:
- tokens: bfloat16 [16384, 2048], P('seq', 'tp'), may hold values from -6 to 6
- key_weight: bfloat16 [2048, 2048], P(None, 'tp'), may hold values from -0.125 to 0.125
- value_weight: bfloat16 [2048, 2048], P(None, 'tp'), may hold values from -0.125 to 0.125
- queries: bfloat16 [16384, 2, 2048], P('seq', None, 'tp'), may hold values from -256 to 256
- prompt_pages: int32 [16], replicated, may hold values from 1 to 97, 1024 in all
- page_table: int32 [1024], P('seq'), may hold values from 0 to 1023, as said below
Outputs:
- attended: bfloat16 [16384, 2, 2048], P('seq', None, 'tp')
- cache: bfloat16 [1024, 16, 2, 2048], P('seq', None, None, 'tp')
Inputs may be any that keep to these rules, and one draw needn't show every extreme that they name: `prompt_pages`: lengths of the prompts in pages; they sum to 1024 and the longest has exactly 97 pages. `page_table`: A permutation of the cache pages. Page c is held by owner c // 16 of seq. At most 1 pages of one stream block go to one owner, some block sends exactly 1 to one owner, and every owner receives 256/16 pages.
All inputs are finite; a program needn't handle non-finite values.
Results may differ from a plain program's by a relative error of at most 0.03.
Values may be sent and summed in bfloat16 or wider, within the bound.
No kernel may reach another device: no remote copies, remote signals or barrier semaphores. Data moves between devices by JAX's collectives and lax.ppermute only.
A program may use at most 64 MiB of HBM per device.

v0:
```python
import math
import jax
import jax.numpy as jnp
from jax import lax
from jax.sharding import PartitionSpec as P

HD = 128
TOPK = 2
PAGE = 16
BACK = 6


def from_behind(value, axis, by):
    peers = lax.axis_size(axis)
    pairs = [(i, i + by) for i in range(peers) if 0 <= i + by < peers]
    return lax.ppermute(value, axis, pairs)


def segment_info(positions, prompt_pages):
    ends = PAGE * jnp.cumsum(prompt_pages)
    below = ends[None, :] <= positions[:, None]
    segment = jnp.sum(below.astype(jnp.int32), axis=1)
    start = jnp.max(jnp.where(below, ends[None, :], 0), axis=1)
    return (segment, positions - start)


def rotate_heads(raw, offsets):
    half = HD // 2
    inverse = 10000.0 ** (-(2.0 * jnp.arange(half, dtype=jnp.float32)) / HD)
    angle = offsets.astype(jnp.float32)[:, None] * inverse[None, :]
    cosine = jnp.cos(angle)[:, None, :]
    sine = jnp.sin(angle)[:, None, :]
    lower = raw[..., :half]
    upper = raw[..., half:]
    return jnp.concatenate([lower * cosine - upper * sine, upper * cosine + lower * sine], axis=-1)


def body(tokens, key_weight, value_weight, queries, prompt_pages, page_table):
    block_rows = tokens.shape[0]
    width = key_weight.shape[1]
    local_heads = width // HD
    devices = lax.axis_size("seq")
    first_row = lax.axis_index("seq") * block_rows
    positions = first_row + jnp.arange(block_rows, dtype=jnp.int32)
    segment, offsets = segment_info(positions, prompt_pages)
    piece = lax.all_gather(tokens, "tp", axis=1, tiled=True)
    raw_keys = jnp.dot(piece, key_weight, preferred_element_type=jnp.float32)
    raw_values = jnp.dot(piece, value_weight, preferred_element_type=jnp.float32)
    keys = rotate_heads(raw_keys.reshape(block_rows, local_heads, HD), offsets).astype(jnp.bfloat16)
    values = raw_values.astype(jnp.bfloat16)
    key_value = jnp.stack([keys.reshape(block_rows, width), values], axis=1)
    blocks = [key_value]
    previous = key_value
    for distance in range(1, BACK + 1):
        previous = from_behind(previous, "seq", 1)
        blocks.append(previous)
    query = queries.reshape(block_rows, TOPK, local_heads, HD)
    scale = 1.0 / math.sqrt(HD)
    masks = []
    for distance in range(BACK + 1):
        key_place = positions - distance * block_rows
        key_segment, unused_offsets = segment_info(key_place, prompt_pages)
        allowed = (segment[:, None] == key_segment[None, :]) & (
            key_place[None, :] <= positions[:, None]
        )
        masks.append(allowed & (key_place[None, :] >= 0))

    def block_scores(expert_query, block, allowed):
        key_heads = block[:, 0].reshape(block_rows, local_heads, HD)
        scores = (
            jnp.einsum("qhd,khd->qhk", expert_query, key_heads, preferred_element_type=jnp.float32)
            * scale
        )
        return jnp.where(allowed[:, None, :], scores, -jnp.inf)

    outputs = []
    for expert in range(TOPK):
        expert_query = query[:, expert]
        score_list = []
        for distance in range(BACK + 1):
            block = blocks[distance]
            allowed = masks[distance]

            def compute(block=block, allowed=allowed):
                return block_scores(expert_query, block, allowed)

            score_list.append(compute())
        peak = jnp.max(score_list[0], axis=-1)
        for distance in range(1, BACK + 1):
            peak = jnp.maximum(peak, jnp.max(score_list[distance], axis=-1))
        total = jnp.zeros((block_rows, local_heads), jnp.float32)
        summed = jnp.zeros((block_rows, local_heads, HD), jnp.float32)
        for distance in range(BACK + 1):
            block = blocks[distance]
            allowed = masks[distance]
            scores = score_list[distance]

            def accumulate(state, block=block, scores=scores):
                weight = jnp.exp(scores - peak[..., None])
                rounded = weight.astype(jnp.bfloat16)
                value_heads = block[:, 1].reshape(block_rows, local_heads, HD)
                product = jnp.einsum(
                    "qhk,khd->qhd", rounded, value_heads, preferred_element_type=jnp.float32
                )
                return (state[0] + jnp.sum(weight, axis=-1), state[1] + product)

            total, summed = accumulate((total, summed))
        outputs.append((summed / total[..., None]).astype(jnp.bfloat16))
    attended = jnp.stack(outputs, axis=1).reshape(block_rows, TOPK, width)
    pages_dev = block_rows // PAGE
    capacity = max(1, pages_dev // devices)
    page_data = key_value.reshape(pages_dev, PAGE * 2 * width)
    owner = page_table // pages_dev
    place_on_owner = page_table % pages_dev
    page_order = jnp.arange(pages_dev, dtype=jnp.int32)
    earlier = (owner[:, None] == owner[None, :]) & (page_order[None, :] < page_order[:, None])
    rank = jnp.sum(earlier.astype(jnp.int32), axis=1)
    target = (owner[None, None, :] == jnp.arange(devices, dtype=jnp.int32)[:, None, None]) & (
        rank[None, None, :] == jnp.arange(capacity, dtype=jnp.int32)[None, :, None]
    )
    outgoing = jnp.einsum(
        "dcp,pf->dcf", target.astype(jnp.bfloat16), page_data, preferred_element_type=jnp.float32
    ).astype(jnp.bfloat16)
    labels = jnp.sum(jnp.where(target, place_on_owner[None, None, :] + 1, 0), axis=2) - 1
    incoming, arrived = (
        lax.all_to_all(outgoing, "seq", split_axis=0, concat_axis=0, tiled=True),
        lax.all_to_all(labels, "seq", split_axis=0, concat_axis=0, tiled=True),
    )
    placing = (arrived.reshape(-1)[None, :] == page_order[:, None]).astype(jnp.bfloat16)
    pool = jnp.dot(
        placing,
        incoming.reshape(devices * capacity, PAGE * 2 * width),
        preferred_element_type=jnp.float32,
    ).astype(jnp.bfloat16)
    cache = pool.reshape(pages_dev, PAGE, 2, width)
    return (attended, cache)


def solution(mesh):
    in_specs = (P("seq", "tp"), P(None, "tp"), P(None, "tp"), P("seq", None, "tp"), P(), P("seq"))
    out_specs = (P("seq", None, "tp"), P("seq", None, None, "tp"))
    return jax.shard_map(body, mesh=mesh, in_specs=in_specs, out_specs=out_specs, check_vma=False)
```

profile of v0, /device:TPU:6, one launch (start us, length us, event | category | flops | bytes accessed | tf_op | source)
XLA Modules:
  0.0 179.1 jit_solution(18239066020747687075)
XLA Ops:
  9.6 12.6 %all-to-all-start = ((s32[64,1,1]{2,1,0:T(1,128)}), s32[64,1,1]{2,1,0:T(1,128)S(1)}, u32[]{:S(2)}, u32[]{:S(2)}) async-start(s32[64,1,1]{2,1,0:T(1,128)} %copy.187), calls=%async_computation | async-start | bytes 65536 | tf_op jit(solution)/shard_map/all_to_all | solution.py:127
  23.9 2.1 %and_and_fusion.5 = (pred[256,256]{0,1:T(8,128)(4,1)}, pred[256,256]{0,1:T(8,128)(4,1)}, pred[256,256]{0,1:T(8,128)(4,1)}, pred[256,256]{0,1:T(8,128)(4,1)}, pre...) fusion(s32[256]{0:T(256)S(1)} %get-tuple-element.80, s32[256]{0:T(256)S(1)} %get-tuple-element.25, s32[256]{0:T(256)S(1)} %fusion.110, ...), kind=kLoop, calls=%fused_computation.134 | loop fusion | flops 1572864 | bytes 407040 | tf_op jit(solution)/shard_map/and | solution.py:66
  27.9 2.7 %all-to-all-done = s32[64,1,1]{2,1,0:T(1,128)S(1)} async-done(((s32[64,1,1]{2,1,0:T(1,128)}), s32[64,1,1]{2,1,0:T(1,128)S(1)}, u32[]{:S(2)}, u32[]{:S(2)}) %all-to-all-start) | async-done | bytes 288 | tf_op jit(solution)/shard_map/all_to_all | solution.py:127
  30.6 1.8 %reduce.2 = s32[64]{0:T(128)} reduce(s32[64,1,1]{2,1,0:T(1,128)S(1)} %all-to-all-done, s32[]{:T(128)} %constant.64.clone.1), dimensions={1,2}, to_apply=%all_to_all.7.reduce_sub_computation | reduce | bytes 516 | tf_op jit(solution)/shard_map/all_to_all | solution.py:127
  32.4 16.9 %all-gather.2.cloned.1.call-done = bf16[256,2048]{1,0:T(8,128)(2,1)} async-done(((bf16[256,256]{1,0:T(8,128)(2,1)}), bf16[256,2048]{1,0:T(8,128)(2,1)}) %all-gather.2.cloned.1.call-update) | async-done | bytes 1048592 | tf_op jit(solution)/shard_map/all_gather | solution.py:46
  49.2 1.7 fusion.134
  52.3 1.7 convolution_convert_fusion.2
  54.7 3.4 %collective-permute-start = (bf16[256,2,256]{0,2,1:T(8,128)(2,1)}, bf16[256,2,256]{0,2,1:T(8,128)(2,1)}, u32[]{:S(2)}, u32[]{:S(2)}) collective-permute-start(bf16[256,2,256]{0,2,1:T(8,128)(2,1)} %pad_maximum_fusion), channel_id=1, source_target_pairs={{0,8},{8,16},{16,24},{24,32},{32,40},{40,48},{48,56},{56,64},{64,7... | collective-permute-start | bytes 786440 | tf_op jit(solution)/shard_map/ppermute | solution.py:16
  62.0 1.6 reshape.847
  63.6 9.9 %all-to-all-start.1 = ((bf16[64,2,4096]{2,1,0:T(2,128)(2,1)}), bf16[64,2,4096]{2,1,0:T(2,128)(2,1)}, u32[]{:S(2)}, u32[]{:S(2)}) async-start(bf16[64,2,4096]{2,1,0:T(2,128)(2,1)} %reshape.847), calls=%async_computation.1 | async-start | bytes 2097152 | tf_op jit(solution)/shard_map/all_to_all | solution.py:126
  75.4 3.4 %collective-permute-start.1 = (bf16[256,2,256]{0,2,1:T(8,128)(2,1)}, bf16[256,2,256]{0,2,1:T(8,128)(2,1)S(1)}, u32[]{:S(2)}, u32[]{:S(2)}) collective-permute-start(bf16[256,2,256]{0,2,1:T(8,128)(2,1)} %collective-permute-done), channel_id=1, source_target_pairs={{0,8},{8,16},{16,24},{24,32},{32,40},{40,48},{48,56},{56,64},{64,7... | collective-permute-start | bytes 786440 | tf_op jit(solution)/shard_map/ppermute | solution.py:16
  80.3 25.0 %collective-permute-done.1 = bf16[256,2,256]{0,2,1:T(8,128)(2,1)S(1)} collective-permute-done((bf16[256,2,256]{0,2,1:T(8,128)(2,1)}, bf16[256,2,256]{0,2,1:T(8,128)(2,1)S(1)}, u32[]{:S(2)}, u32[]{:S(2)}) %collective-permute-start.1) | collective-permute-done | bytes 262176 | tf_op jit(solution)/shard_map/ppermute | solution.py:16
  105.3 1.9 %collective-permute-start.2 = (bf16[256,2,256]{0,2,1:T(8,128)(2,1)S(1)}, bf16[256,2,256]{0,2,1:T(8,128)(2,1)S(1)}, u32[]{:S(2)}, u32[]{:S(2)}) collective-permute-start(bf16[256,2,256]{0,2,1:T(8,128)(2,1)S(1)} %collective-permute-done.1), channel_id=1, source_target_pairs={{0,8},{8,16},{16,24},{24,32},{32,40},{40,48},{48,56},{56,64},{64,7... | collective-permute-start | bytes 786440 | tf_op jit(solution)/shard_map/ppermute | solution.py:16
  107.9 9.7 %collective-permute-done.2 = bf16[256,2,256]{0,2,1:T(8,128)(2,1)S(1)} collective-permute-done((bf16[256,2,256]{0,2,1:T(8,128)(2,1)S(1)}, bf16[256,2,256]{0,2,1:T(8,128)(2,1)S(1)}, u32[]{:S(2)}, u32[]{:S(2)}) %collective-permute-start.2) | collective-permute-done | bytes 262176 | tf_op jit(solution)/shard_map/ppermute | solution.py:16
  117.6 1.9 %collective-permute-start.3 = (bf16[256,2,256]{0,2,1:T(8,128)(2,1)S(1)}, bf16[256,2,256]{0,2,1:T(8,128)(2,1)S(1)}, u32[]{:S(2)}, u32[]{:S(2)}) collective-permute-start(bf16[256,2,256]{0,2,1:T(8,128)(2,1)S(1)} %collective-permute-done.2), channel_id=1, source_target_pairs={{0,8},{8,16},{16,24},{24,32},{32,40},{40,48},{48,56},{56,64},{64,7... | collective-permute-start | bytes 786440 | tf_op jit(solution)/shard_map/ppermute | solution.py:16
  120.1 8.8 %collective-permute-done.3 = bf16[256,2,256]{0,2,1:T(8,128)(2,1)S(1)} collective-permute-done((bf16[256,2,256]{0,2,1:T(8,128)(2,1)S(1)}, bf16[256,2,256]{0,2,1:T(8,128)(2,1)S(1)}, u32[]{:S(2)}, u32[]{:S(2)}) %collective-permute-start.3) | collective-permute-done | bytes 262176 | tf_op jit(solution)/shard_map/ppermute | solution.py:16
  128.9 1.9 %collective-permute-start.4 = (bf16[256,2,256]{0,2,1:T(8,128)(2,1)S(1)}, bf16[256,2,256]{0,2,1:T(8,128)(2,1)S(1)}, u32[]{:S(2)}, u32[]{:S(2)}) collective-permute-start(bf16[256,2,256]{0,2,1:T(8,128)(2,1)S(1)} %collective-permute-done.3), channel_id=1, source_target_pairs={{0,8},{8,16},{16,24},{24,32},{32,40},{40,48},{48,56},{56,64},{64,7... | collective-permute-start | bytes 786440 | tf_op jit(solution)/shard_map/ppermute | solution.py:16
  131.5 8.7 %collective-permute-done.4 = bf16[256,2,256]{0,2,1:T(8,128)(2,1)S(1)} collective-permute-done((bf16[256,2,256]{0,2,1:T(8,128)(2,1)S(1)}, bf16[256,2,256]{0,2,1:T(8,128)(2,1)S(1)}, u32[]{:S(2)}, u32[]{:S(2)}) %collective-permute-start.4) | collective-permute-done | bytes 262176 | tf_op jit(solution)/shard_map/ppermute | solution.py:16
  140.2 2.1 %collective-permute-start.5 = (bf16[256,2,256]{0,2,1:T(8,128)(2,1)S(1)}, bf16[256,2,256]{0,2,1:T(8,128)(2,1)S(1)}, u32[]{:S(2)}, u32[]{:S(2)}) collective-permute-start(bf16[256,2,256]{0,2,1:T(8,128)(2,1)S(1)} %collective-permute-done.4), channel_id=1, source_target_pairs={{0,8},{8,16},{16,24},{24,32},{32,40},{40,48},{48,56},{56,64},{64,7... | collective-permute-start | bytes 786440 | tf_op jit(solution)/shard_map/ppermute | solution.py:16
  142.6 1.7 fusion.121
  144.3 7.2 %collective-permute-done.5 = bf16[256,2,256]{0,2,1:T(8,128)(2,1)S(1)} collective-permute-done((bf16[256,2,256]{0,2,1:T(8,128)(2,1)S(1)}, bf16[256,2,256]{0,2,1:T(8,128)(2,1)S(1)}, u32[]{:S(2)}, u32[]{:S(2)}) %collective-permute-start.5) | collective-permute-done | bytes 262176 | tf_op jit(solution)/shard_map/ppermute | solution.py:16
  151.8 1.7 fusion.120
  158.3 1.9 %fusion.53 = (f32[256,2]{0,1:T(2,128)S(1)}, f32[256,2]{0,1:T(2,128)S(1)}, f32[256,2]{0,1:T(2,128)S(1)}, f32[256,2]{0,1:T(2,128)S(1)}, f32[256,2]{0,1:T(2,128)S(1...) fusion(f32[256,2,256]{0,2,1:T(8,128)S(1)} %get-tuple-element.65, f32[256,2]{0,1:T(2,128)S(1)} %maximum_maximum_fusion, ...), kind=kLoop, calls=%fused_computation.96 | loop fusion | flops 1831424 | bytes 3686400 | tf_op jit(solution)/shard_map/reduce_sum | solution.py:105
  163.6 6.5 %reshape.848 = bf16[64,1,8192]{2,1,0:T(2,128)(2,1)S(1)} reshape(bf16[64,2,4096]{2,1,0:T(2,128)(2,1)} %all-to-all-done.1) | data formatting | bytes 2097152
  (135 shorter events, 27.6 us)
Async XLA Ops:
  7.2 42.1 %copy-start = (bf16[2048,256]{1,0:T(8,128)(2,1)S(1)}, bf16[2048,256]{1,0:T(8,128)(2,1)}, u32[]{:S(2)}) copy-start(bf16[2048,256]{1,0:T(8,128)(2,1)} %param.7) | copy-start | bytes 3145732
  7.2 42.0 %all-gather.2.cloned.1.call-start = ((), (), s32[]{:S(2)}) async-start(), calls=%async_computation.2 | async-start | bytes 1179648 | tf_op jit(solution)/shard_map/all_gather | solution.py:46
  9.6 21.0 %all-to-all-start = ((s32[64,1,1]{2,1,0:T(1,128)}), s32[64,1,1]{2,1,0:T(1,128)S(1)}, u32[]{:S(2)}, u32[]{:S(2)}) async-start(s32[64,1,1]{2,1,0:T(1,128)} %copy.187), calls=%async_computation | async-start | bytes 65536 | tf_op jit(solution)/shard_map/all_to_all | solution.py:127
  54.7 20.6 %collective-permute-start = (bf16[256,2,256]{0,2,1:T(8,128)(2,1)}, bf16[256,2,256]{0,2,1:T(8,128)(2,1)}, u32[]{:S(2)}, u32[]{:S(2)}) collective-permute-start(bf16[256,2,256]{0,2,1:T(8,128)(2,1)} %pad_maximum_fusion), channel_id=1, source_target_pairs={{0,8},{8,16},{16,24},{24,32},{32,40},{40,48},{48,56},{56,64},{64,7... | collective-permute-start | bytes 786440 | tf_op jit(solution)/shard_map/ppermute | solution.py:16
  62.0 11.5 %copy-start.22 = (bf16[256,2,128]{2,0,1:T(8,128)(2,1)S(1)}, bf16[256,2,128]{2,0,1:T(8,128)(2,1)}, u32[]{:S(2)}) copy-start(bf16[256,2,128]{2,0,1:T(8,128)(2,1)} %copy-done.21) | copy-start | bytes 393220
  62.0 11.5 %copy-start.25 = (pred[256,256]{0,1:T(8,128)(4,1)S(1)}, pred[256,256]{0,1:T(8,128)(4,1)}, u32[]{:S(2)}) copy-start(pred[256,256]{0,1:T(8,128)(4,1)} %get-tuple-element.47) | copy-start | bytes 196612
  63.6 16.1 %copy-start.19 = (pred[256,256]{0,1:T(8,128)(4,1)S(1)}, pred[256,256]{0,1:T(8,128)(4,1)}, u32[]{:S(2)}) copy-start(pred[256,256]{0,1:T(8,128)(4,1)} %get-tuple-element.42) | copy-start | bytes 196612
  63.6 100.0 %all-to-all-start.1 = ((bf16[64,2,4096]{2,1,0:T(2,128)(2,1)}), bf16[64,2,4096]{2,1,0:T(2,128)(2,1)}, u32[]{:S(2)}, u32[]{:S(2)}) async-start(bf16[64,2,4096]{2,1,0:T(2,128)(2,1)} %reshape.847), calls=%async_computation.1 | async-start | bytes 2097152 | tf_op jit(solution)/shard_map/all_to_all | solution.py:126
  73.5 33.8 %copy-start.20 = (pred[256,256]{0,1:T(8,128)(4,1)S(1)}, pred[256,256]{0,1:T(8,128)(4,1)}, u32[]{:S(2)}) copy-start(pred[256,256]{0,1:T(8,128)(4,1)} %and_and_fusion.4) | copy-start | bytes 196612
  75.4 30.0 %collective-permute-start.1 = (bf16[256,2,256]{0,2,1:T(8,128)(2,1)}, bf16[256,2,256]{0,2,1:T(8,128)(2,1)S(1)}, u32[]{:S(2)}, u32[]{:S(2)}) collective-permute-start(bf16[256,2,256]{0,2,1:T(8,128)(2,1)} %collective-permute-done), channel_id=1, source_target_pairs={{0,8},{8,16},{16,24},{24,32},{32,40},{40,48},{48,56},{56,64},{64,7... | collective-permute-start | bytes 786440 | tf_op jit(solution)/shard_map/ppermute | solution.py:16
  79.7 74.0 %copy-start.5 = (bf16[256,1,256]{0,2,1:T(8,128)(2,1)}, bf16[256,1,256]{0,2,1:T(8,128)(2,1)S(1)}, u32[]{:S(2)}) copy-start(bf16[256,1,256]{0,2,1:T(8,128)(2,1)S(1)} %get-tuple-element.38) | copy-start | bytes 393220
  79.7 39.8 %copy-start.18 = (pred[256,256]{0,1:T(8,128)(4,1)S(1)}, pred[256,256]{0,1:T(8,128)(4,1)}, u32[]{:S(2)}) copy-start(pred[256,256]{0,1:T(8,128)(4,1)} %get-tuple-element.46) | copy-start | bytes 196612
  105.3 12.2 %collective-permute-start.2 = (bf16[256,2,256]{0,2,1:T(8,128)(2,1)S(1)}, bf16[256,2,256]{0,2,1:T(8,128)(2,1)S(1)}, u32[]{:S(2)}, u32[]{:S(2)}) collective-permute-start(bf16[256,2,256]{0,2,1:T(8,128)(2,1)S(1)} %collective-permute-done.1), channel_id=1, source_target_pairs={{0,8},{8,16},{16,24},{24,32},{32,40},{40,48},{48,56},{56,64},{64,7... | collective-permute-start | bytes 786440 | tf_op jit(solution)/shard_map/ppermute | solution.py:16
  107.3 46.7 %copy-start.7 = (bf16[256,1,256]{0,2,1:T(8,128)(2,1)}, bf16[256,1,256]{0,2,1:T(8,128)(2,1)S(1)}, u32[]{:S(2)}) copy-start(bf16[256,1,256]{0,2,1:T(8,128)(2,1)S(1)} %get-tuple-element.36) | copy-start | bytes 393220
  107.3 23.6 %copy-start.17 = (pred[256,256]{0,1:T(8,128)(4,1)S(1)}, pred[256,256]{0,1:T(8,128)(4,1)}, u32[]{:S(2)}) copy-start(pred[256,256]{0,1:T(8,128)(4,1)} %get-tuple-element.43) | copy-start | bytes 196612
  117.6 11.4 %collective-permute-start.3 = (bf16[256,2,256]{0,2,1:T(8,128)(2,1)S(1)}, bf16[256,2,256]{0,2,1:T(8,128)(2,1)S(1)}, u32[]{:S(2)}, u32[]{:S(2)}) collective-permute-start(bf16[256,2,256]{0,2,1:T(8,128)(2,1)S(1)} %collective-permute-done.2), channel_id=1, source_target_pairs={{0,8},{8,16},{16,24},{24,32},{32,40},{40,48},{48,56},{56,64},{64,7... | collective-permute-start | bytes 786440 | tf_op jit(solution)/shard_map/ppermute | solution.py:16
  119.5 34.7 %copy-start.9 = (bf16[256,1,256]{0,2,1:T(8,128)(2,1)}, bf16[256,1,256]{0,2,1:T(8,128)(2,1)S(1)}, u32[]{:S(2)}) copy-start(bf16[256,1,256]{0,2,1:T(8,128)(2,1)S(1)} %get-tuple-element.34) | copy-start | bytes 393220
  119.5 22.8 %copy-start.16 = (pred[256,256]{0,1:T(8,128)(4,1)S(1)}, pred[256,256]{0,1:T(8,128)(4,1)}, u32[]{:S(2)}) copy-start(pred[256,256]{0,1:T(8,128)(4,1)} %get-tuple-element.44) | copy-start | bytes 196612
  128.9 11.3 %collective-permute-start.4 = (bf16[256,2,256]{0,2,1:T(8,128)(2,1)S(1)}, bf16[256,2,256]{0,2,1:T(8,128)(2,1)S(1)}, u32[]{:S(2)}, u32[]{:S(2)}) collective-permute-start(bf16[256,2,256]{0,2,1:T(8,128)(2,1)S(1)} %collective-permute-done.3), channel_id=1, source_target_pairs={{0,8},{8,16},{16,24},{24,32},{32,40},{40,48},{48,56},{56,64},{64,7... | collective-permute-start | bytes 786440 | tf_op jit(solution)/shard_map/ppermute | solution.py:16
  130.9 24.1 %copy-start.11 = (bf16[256,1,256]{0,2,1:T(8,128)(2,1)}, bf16[256,1,256]{0,2,1:T(8,128)(2,1)S(1)}, u32[]{:S(2)}) copy-start(bf16[256,1,256]{0,2,1:T(8,128)(2,1)S(1)} %get-tuple-element.32) | copy-start | bytes 393220
  130.9 20.6 %copy-start.15 = (pred[256,256]{0,1:T(8,128)(4,1)S(1)}, pred[256,256]{0,1:T(8,128)(4,1)}, u32[]{:S(2)}) copy-start(pred[256,256]{0,1:T(8,128)(4,1)} %get-tuple-element.45) | copy-start | bytes 196612
  140.2 11.3 %collective-permute-start.5 = (bf16[256,2,256]{0,2,1:T(8,128)(2,1)S(1)}, bf16[256,2,256]{0,2,1:T(8,128)(2,1)S(1)}, u32[]{:S(2)}, u32[]{:S(2)}) collective-permute-start(bf16[256,2,256]{0,2,1:T(8,128)(2,1)S(1)} %collective-permute-done.4), channel_id=1, source_target_pairs={{0,8},{8,16},{16,24},{24,32},{32,40},{40,48},{48,56},{56,64},{64,7... | collective-permute-start | bytes 786440 | tf_op jit(solution)/shard_map/ppermute | solution.py:16
  142.3 12.9 %copy-start.13 = (bf16[256,1,256]{0,2,1:T(8,128)(2,1)}, bf16[256,1,256]{0,2,1:T(8,128)(2,1)S(1)}, u32[]{:S(2)}) copy-start(bf16[256,1,256]{0,2,1:T(8,128)(2,1)S(1)} %get-tuple-element.30) | copy-start | bytes 393220
  162.1 8.0 %copy-start.26 = (s32[64]{0:T(128)S(1)}, s32[64]{0:T(128)}, u32[]{:S(2)}) copy-start(s32[64]{0:T(128)} %reduce.2) | copy-start | bytes 772
  (12 other events, 19.9 us)
Sparse Core Ops, SparseCore 0:
  10.1 39.0 all-gather.1
where the time goes:
time: 180 us; the launch traced here: 179 us
  waiting for transfers between devices  79.6 us (44%)
  starting transfers between devices  37.1 us (21%)
  matrix products  17.2 us (10%)
  local copies, waits for them, and re-layouts  17 us (9%)
  between operations  14.8 us (8%)
  other arithmetic  13.3 us (7%)
    ppermute x6, waiting for transfers between devices, from_behind(): return lax.ppermute(value, axis, pairs)  59.4 us
    all_gather x1, waiting for transfers between devices, body(): piece = lax.all_gather(tokens, 'tp', axis=1, tiled=True)  16.9 us
    ppermute x6, starting transfers between devices, from_behind(): return lax.ppermute(value, axis, pairs)  14.6 us
    all_to_all x1, starting transfers between devices, body(): lax.all_to_all(labels, 'seq', split_axis=0, concat_axis=0, tiled=True)  12.6 us
    unnamed x59, local copies, waits for them, and re-layouts  10.3 us
    all_to_all x1, starting transfers between devices, body(): lax.all_to_all(outgoing, 'seq', split_axis=0, concat_axis=0, tiled=True)  9.87 us
    dot_general x14, matrix products, block_scores(): jnp.einsum('qhd,khd->qhk', expert_query, key_heads, preferred_element_typ...  8.03 us
    dot_general x14, matrix products, accumulate(): jnp.einsum('qhk,khd->qhd', rounded, value_heads, preferred_element_type=j...  3.92 us
  transfers between devices with their start and end apart: 9, of which 7 were waited for; matrix products, arithmetic and copies ran while one was open for 19% of the time, Pallas kernels for 0%

commit v1 on v0

--- a/solution.py
+++ b/solution.py
@@ -43,7 +43,9 @@
     first_row = lax.axis_index("seq") * block_rows
     positions = first_row + jnp.arange(block_rows, dtype=jnp.int32)
     segment, offsets = segment_info(positions, prompt_pages)
-    piece = lax.all_gather(tokens, "tp", axis=1, tiled=True)
+    piece = jnp.concatenate(
+        lax.all_to_all(jnp.stack([tokens] * lax.axis_size("tp")), "tp", 0, 0), axis=1
+    )
     raw_keys = jnp.dot(piece, key_weight, preferred_element_type=jnp.float32)
     raw_values = jnp.dot(piece, value_weight, preferred_element_type=jnp.float32)
     keys = rotate_heads(raw_keys.reshape(block_rows, local_heads, HD), offsets).astype(jnp.bfloat16)

time: 180 us -> 187 us (1.039)
  between operations: 14.8 us -> 1.44 us
  local copies, waits for them, and re-layouts: 17 us -> 25.3 us
  starting transfers between devices: 37.1 us -> 45.2 us
  waiting for transfers between devices: 79.6 us -> 85 us
  matrix products: 17.2 us -> 14.9 us
    all_to_all x0 -> x1, waiting for transfers between devices: none -> 20.3 us  [body(): lax.all_to_all(jnp.stack([tokens] * lax.axis_size('tp')), 'tp', 0, 0)]
    all_gather x1 -> x0, waiting for transfers between devices: 16.9 us -> none  [body(): piece = lax.all_gather(tokens, 'tp', axis=1, tiled=True)]
    all_to_all x0 -> x1, starting transfers between devices: none -> 9.41 us  [body(): lax.all_to_all(jnp.stack([tokens] * lax.axis_size('tp')), 'tp', 0, 0)]
    all_to_all x1, waiting for transfers between devices: 2.7 us -> 8.31 us  [body(): lax.all_to_all(labels, 'seq', split_axis=0, concat_axis=0, tiled=True)]
    reshape x0 -> x3, local copies, waits for them, and re-layouts: none -> 4.04 us  [body(): jnp.concatenate(lax.all_to_all(jnp.stack([tokens] * lax.axis_size('tp')),...]
    ppermute x6, waiting for transfers between devices: 59.4 us -> 56.4 us  [from_behind(): return lax.ppermute(value, axis, pairs)]
    unnamed x59 -> x67, local copies, waits for them, and re-layouts: 10.3 us -> 11.2 us
  transfers between devices with their start and end apart: 9 -> 9, of which waited for: 7 -> 7; matrix products, arithmetic and copies ran while one was open for 19% -> 18% of each run, Pallas kernels for 0% -> 0%
where the time goes in v1:
time: 187 us; the launch traced here: 186 us
  waiting for transfers between devices  85 us (45%)
  starting transfers between devices  45.2 us (24%)
  local copies, waits for them, and re-layouts  25.3 us (14%)
  matrix products  14.9 us (8%)
  other arithmetic  13.7 us (7%)
    ppermute x6, waiting for transfers between devices, from_behind(): return lax.ppermute(value, axis, pairs)  56.4 us
    all_to_all x1, waiting for transfers between devices, body(): lax.all_to_all(jnp.stack([tokens] * lax.axis_size('tp')), 'tp', 0, 0)  20.3 us
    ppermute x6, starting transfers between devices, from_behind(): return lax.ppermute(value, axis, pairs)  13.7 us
    all_to_all x1, starting transfers between devices, body(): lax.all_to_all(labels, 'seq', split_axis=0, concat_axis=0, tiled=True)  12.6 us
    unnamed x67, local copies, waits for them, and re-layouts  11.2 us
    all_to_all x1, starting transfers between devices, body(): lax.all_to_all(outgoing, 'seq', split_axis=0, concat_axis=0, tiled=True)  9.46 us
    all_to_all x1, starting transfers between devices, body(): lax.all_to_all(jnp.stack([tokens] * lax.axis_size('tp')), 'tp', 0, 0)  9.41 us
    all_to_all x1, waiting for transfers between devices, body(): lax.all_to_all(labels, 'seq', split_axis=0, concat_axis=0, tiled=True)  8.31 us
  transfers between devices with their start and end apart: 9, of which 7 were waited for; matrix products, arithmetic and copies ran while one was open for 18% of the time, Pallas kernels for 0%

profile of v1, /device:TPU:6, one launch (start us, length us, event | category | flops | bytes accessed | tf_op | source)
XLA Modules:
  0.0 185.6 jit_solution(3967922898008019957)
XLA Ops:
  2.4 12.6 %all-to-all-start.1 = ((s32[64,1,1]{2,1,0:T(1,128)}), s32[64,1,1]{2,1,0:T(1,128)S(1)}, u32[]{:S(2)}, u32[]{:S(2)}) async-start(s32[64,1,1]{2,1,0:T(1,128)} %copy.190), calls=%async_computation.1 | async-start | bytes 65536 | tf_op jit(solution)/shard_map/all_to_all | solution.py:129
  15.1 8.3 %all-to-all-done.1 = s32[64,1,1]{2,1,0:T(1,128)S(1)} async-done(((s32[64,1,1]{2,1,0:T(1,128)}), s32[64,1,1]{2,1,0:T(1,128)S(1)}, u32[]{:S(2)}, u32[]{:S(2)}) %all-to-all-start.1) | async-done | bytes 288 | tf_op jit(solution)/shard_map/all_to_all | solution.py:129
  23.4 2.0 %stack.12 = bf16[8,256,256]{2,1,0:T(8,128)(2,1)} broadcast(bf16[256,256]{1,0:T(8,128)(2,1)} %param.6), dimensions={1,2} | broadcast | bytes 1179648 | tf_op jit(solution)/shard_map/stack | solution.py:47
  25.4 9.4 %all-to-all-start = ((bf16[8,256,256]{2,1,0:T(8,128)(2,1)}), bf16[8,256,256]{2,1,0:T(8,128)(2,1)S(1)}, u32[]{:S(2)}, u32[]{:S(2)}) async-start(bf16[8,256,256]{2,1,0:T(8,128)(2,1)} %stack.12), calls=%async_computation | async-start | bytes 2097152 | tf_op jit(solution)/shard_map/all_to_all | solution.py:47
  38.9 2.0 %and_and_fusion.5 = (pred[256,256]{0,1:T(8,128)(4,1)}, pred[256,256]{0,1:T(8,128)(4,1)}, pred[256,256]{0,1:T(8,128)(4,1)}, pred[256,256]{0,1:T(8,128)(4,1)}, pre...) fusion(s32[256]{0:T(256)S(1)} %get-tuple-element.78, s32[256]{0:T(256)S(1)} %get-tuple-element.25, s32[256]{0:T(256)S(1)} %fusion.110, ...), kind=kLoop, calls=%fused_computation.132 | loop fusion | flops 1572864 | bytes 407040 | tf_op jit(solution)/shard_map/and | solution.py:68
  40.9 2.5 %reduce.2 = s32[64]{0:T(128)} reduce(s32[64,1,1]{2,1,0:T(1,128)} %copy-done.26, s32[]{:T(128)} %constant.64.clone.1), dimensions={1,2}, to_apply=%all_to_all.11.reduce_sub_computation | reduce | bytes 516 | tf_op jit(solution)/shard_map/all_to_all | solution.py:129
  43.4 20.3 %all-to-all-done = bf16[8,256,256]{2,1,0:T(8,128)(2,1)S(1)} async-done(((bf16[8,256,256]{2,1,0:T(8,128)(2,1)}), bf16[8,256,256]{2,1,0:T(8,128)(2,1)S(1)}, u32[]{:S(2)}, u32[]{:S(2)}) %all-to-all-start) | async-done | bytes 1048608 | tf_op jit(solution)/shard_map/all_to_all | solution.py:47
  65.3 2.3 %reshape.853 = bf16[256,2048,1]{1,0,2:T(8,128)(2,1)} reshape(bf16[256,8,256]{2,1,0:T(8,128)(2,1)} %copy.154) | data formatting | bytes 2097152 | tf_op jit(solution)/shard_map/reshape | solution.py:46
  71.4 2.5 %collective-permute-start = (bf16[256,2,256]{0,2,1:T(8,128)(2,1)}, bf16[256,2,256]{0,2,1:T(8,128)(2,1)}, u32[]{:S(2)}, u32[]{:S(2)}) collective-permute-start(bf16[256,2,256]{0,2,1:T(8,128)(2,1)} %pad_maximum_fusion), channel_id=1, source_target_pairs={{0,8},{8,16},{16,24},{24,32},{32,40},{40,48},{48,56},{56,64},{64,7... | collective-permute-start | bytes 786440 | tf_op jit(solution)/shard_map/ppermute | solution.py:16
  79.5 9.5 %all-to-all-start.2 = ((bf16[64,2,4096]{2,1,0:T(2,128)(2,1)}), bf16[64,2,4096]{2,1,0:T(2,128)(2,1)}, u32[]{:S(2)}, u32[]{:S(2)}) async-start(bf16[64,2,4096]{2,1,0:T(2,128)(2,1)} %reshape.857), calls=%async_computation.2 | async-start | bytes 2097152 | tf_op jit(solution)/shard_map/all_to_all | solution.py:128
  90.9 3.4 %collective-permute-start.1 = (bf16[256,2,256]{0,2,1:T(8,128)(2,1)}, bf16[256,2,256]{0,2,1:T(8,128)(2,1)S(1)}, u32[]{:S(2)}, u32[]{:S(2)}) collective-permute-start(bf16[256,2,256]{0,2,1:T(8,128)(2,1)} %collective-permute-done), channel_id=1, source_target_pairs={{0,8},{8,16},{16,24},{24,32},{32,40},{40,48},{48,56},{56,64},{64,7... | collective-permute-start | bytes 786440 | tf_op jit(solution)/shard_map/ppermute | solution.py:16
  95.9 22.8 %collective-permute-done.1 = bf16[256,2,256]{0,2,1:T(8,128)(2,1)S(1)} collective-permute-done((bf16[256,2,256]{0,2,1:T(8,128)(2,1)}, bf16[256,2,256]{0,2,1:T(8,128)(2,1)S(1)}, u32[]{:S(2)}, u32[]{:S(2)}) %collective-permute-start.1) | collective-permute-done | bytes 262176 | tf_op jit(solution)/shard_map/ppermute | solution.py:16
  118.7 1.9 %collective-permute-start.2 = (bf16[256,2,256]{0,2,1:T(8,128)(2,1)S(1)}, bf16[256,2,256]{0,2,1:T(8,128)(2,1)S(1)}, u32[]{:S(2)}, u32[]{:S(2)}) collective-permute-start(bf16[256,2,256]{0,2,1:T(8,128)(2,1)S(1)} %collective-permute-done.1), channel_id=1, source_target_pairs={{0,8},{8,16},{16,24},{24,32},{32,40},{40,48},{48,56},{56,64},{64,7... | collective-permute-start | bytes 786440 | tf_op jit(solution)/shard_map/ppermute | solution.py:16
  121.2 9.1 %collective-permute-done.2 = bf16[256,2,256]{0,2,1:T(8,128)(2,1)S(1)} collective-permute-done((bf16[256,2,256]{0,2,1:T(8,128)(2,1)S(1)}, bf16[256,2,256]{0,2,1:T(8,128)(2,1)S(1)}, u32[]{:S(2)}, u32[]{:S(2)}) %collective-permute-start.2) | collective-permute-done | bytes 262176 | tf_op jit(solution)/shard_map/ppermute | solution.py:16
  130.3 1.9 %collective-permute-start.3 = (bf16[256,2,256]{0,2,1:T(8,128)(2,1)S(1)}, bf16[256,2,256]{0,2,1:T(8,128)(2,1)S(1)}, u32[]{:S(2)}, u32[]{:S(2)}) collective-permute-start(bf16[256,2,256]{0,2,1:T(8,128)(2,1)S(1)} %collective-permute-done.2), channel_id=1, source_target_pairs={{0,8},{8,16},{16,24},{24,32},{32,40},{40,48},{48,56},{56,64},{64,7... | collective-permute-start | bytes 786440 | tf_op jit(solution)/shard_map/ppermute | solution.py:16
  132.9 8.7 %collective-permute-done.3 = bf16[256,2,256]{0,2,1:T(8,128)(2,1)S(1)} collective-permute-done((bf16[256,2,256]{0,2,1:T(8,128)(2,1)S(1)}, bf16[256,2,256]{0,2,1:T(8,128)(2,1)S(1)}, u32[]{:S(2)}, u32[]{:S(2)}) %collective-permute-start.3) | collective-permute-done | bytes 262176 | tf_op jit(solution)/shard_map/ppermute | solution.py:16
  141.6 1.9 %collective-permute-start.4 = (bf16[256,2,256]{0,2,1:T(8,128)(2,1)S(1)}, bf16[256,2,256]{0,2,1:T(8,128)(2,1)S(1)}, u32[]{:S(2)}, u32[]{:S(2)}) collective-permute-start(bf16[256,2,256]{0,2,1:T(8,128)(2,1)S(1)} %collective-permute-done.3), channel_id=1, source_target_pairs={{0,8},{8,16},{16,24},{24,32},{32,40},{40,48},{48,56},{56,64},{64,7... | collective-permute-start | bytes 786440 | tf_op jit(solution)/shard_map/ppermute | solution.py:16
  144.1 8.7 %collective-permute-done.4 = bf16[256,2,256]{0,2,1:T(8,128)(2,1)S(1)} collective-permute-done((bf16[256,2,256]{0,2,1:T(8,128)(2,1)S(1)}, bf16[256,2,256]{0,2,1:T(8,128)(2,1)S(1)}, u32[]{:S(2)}, u32[]{:S(2)}) %collective-permute-start.4) | collective-permute-done | bytes 262176 | tf_op jit(solution)/shard_map/ppermute | solution.py:16
  152.8 2.1 %collective-permute-start.5 = (bf16[256,2,256]{0,2,1:T(8,128)(2,1)S(1)}, bf16[256,2,256]{0,2,1:T(8,128)(2,1)S(1)}, u32[]{:S(2)}, u32[]{:S(2)}) collective-permute-start(bf16[256,2,256]{0,2,1:T(8,128)(2,1)S(1)} %collective-permute-done.4), channel_id=1, source_target_pairs={{0,8},{8,16},{16,24},{24,32},{32,40},{40,48},{48,56},{56,64},{64,7... | collective-permute-start | bytes 786440 | tf_op jit(solution)/shard_map/ppermute | solution.py:16
  155.3 1.7 fusion.120
  157.0 7.1 %collective-permute-done.5 = bf16[256,2,256]{0,2,1:T(8,128)(2,1)S(1)} collective-permute-done((bf16[256,2,256]{0,2,1:T(8,128)(2,1)S(1)}, bf16[256,2,256]{0,2,1:T(8,128)(2,1)S(1)}, u32[]{:S(2)}, u32[]{:S(2)}) %collective-permute-start.5) | collective-permute-done | bytes 262176 | tf_op jit(solution)/shard_map/ppermute | solution.py:16
  169.0 1.8 copy.188
  171.5 1.9 %fusion.53 = (f32[256,2]{0,1:T(2,128)S(1)}, f32[256,2]{0,1:T(2,128)S(1)}, f32[256,2]{0,1:T(2,128)S(1)}, f32[256,2]{0,1:T(2,128)S(1)}, f32[256,2]{0,1:T(2,128)S(1...) fusion(f32[256,2,256]{0,2,1:T(8,128)S(1)} %get-tuple-element.63, f32[256,2]{0,1:T(2,128)S(1)} %maximum_maximum_fusion, ...), kind=kLoop, calls=%fused_computation.96 | loop fusion | flops 1831424 | bytes 3686400 | tf_op jit(solution)/shard_map/reduce_sum | solution.py:107
  177.0 6.5 %reshape.858 = bf16[64,1,8192]{2,1,0:T(2,128)(2,1)S(1)} reshape(bf16[64,2,4096]{2,1,0:T(2,128)(2,1)} %all-to-all-done.2) | data formatting | bytes 2097152
  (145 shorter events, 33.2 us)
Async XLA Ops:
  0.6 69.5 %copy-start = (bf16[2048,256]{1,0:T(8,128)(2,1)S(1)}, bf16[2048,256]{1,0:T(8,128)(2,1)}, u32[]{:S(2)}) copy-start(bf16[2048,256]{1,0:T(8,128)(2,1)} %param.8) | copy-start | bytes 3145732
  0.6 34.1 %copy-start.31 = (s32[16]{0:T(128)S(1)}, s32[16]{0:T(128)}, u32[]{:S(2)}) copy-start(s32[16]{0:T(128)} %param.10) | copy-start | bytes 196
  2.4 21.0 %all-to-all-start.1 = ((s32[64,1,1]{2,1,0:T(1,128)}), s32[64,1,1]{2,1,0:T(1,128)S(1)}, u32[]{:S(2)}, u32[]{:S(2)}) async-start(s32[64,1,1]{2,1,0:T(1,128)} %copy.190), calls=%async_computation.1 | async-start | bytes 65536 | tf_op jit(solution)/shard_map/all_to_all | solution.py:129
  23.4 13.0 %copy-start.26 = (s32[64,1,1]{2,1,0:T(1,128)}, s32[64,1,1]{2,1,0:T(1,128)S(1)}, u32[]{:S(2)}) copy-start(s32[64,1,1]{2,1,0:T(1,128)S(1)} %all-to-all-done.1) | copy-start | bytes 772
  25.4 38.4 %all-to-all-start = ((bf16[8,256,256]{2,1,0:T(8,128)(2,1)}), bf16[8,256,256]{2,1,0:T(8,128)(2,1)S(1)}, u32[]{:S(2)}, u32[]{:S(2)}) async-start(bf16[8,256,256]{2,1,0:T(8,128)(2,1)} %stack.12), calls=%async_computation | async-start | bytes 2097152 | tf_op jit(solution)/shard_map/all_to_all | solution.py:47
  71.4 19.6 %collective-permute-start = (bf16[256,2,256]{0,2,1:T(8,128)(2,1)}, bf16[256,2,256]{0,2,1:T(8,128)(2,1)}, u32[]{:S(2)}, u32[]{:S(2)}) collective-permute-start(bf16[256,2,256]{0,2,1:T(8,128)(2,1)} %pad_maximum_fusion), channel_id=1, source_target_pairs={{0,8},{8,16},{16,24},{24,32},{32,40},{40,48},{48,56},{56,64},{64,7... | collective-permute-start | bytes 786440 | tf_op jit(solution)/shard_map/ppermute | solution.py:16
  77.8 11.1 %copy-start.23 = (bf16[256,2,64]{0,2,1:T(8,128)(2,1)S(1)}, bf16[256,2,64]{0,2,1:T(8,128)(2,1)}, u32[]{:S(2)}) copy-start(bf16[256,2,64]{0,2,1:T(8,128)(2,1)} %copy-done.22) | copy-start | bytes 196612
  79.5 15.8 %copy-start.20 = (pred[256,256]{0,1:T(8,128)(4,1)S(1)}, pred[256,256]{0,1:T(8,128)(4,1)}, u32[]{:S(2)}) copy-start(pred[256,256]{0,1:T(8,128)(4,1)} %get-tuple-element.40) | copy-start | bytes 196612
  79.5 97.5 %all-to-all-start.2 = ((bf16[64,2,4096]{2,1,0:T(2,128)(2,1)}), bf16[64,2,4096]{2,1,0:T(2,128)(2,1)}, u32[]{:S(2)}, u32[]{:S(2)}) async-start(bf16[64,2,4096]{2,1,0:T(2,128)(2,1)} %reshape.857), calls=%async_computation.2 | async-start | bytes 2097152 | tf_op jit(solution)/shard_map/all_to_all | solution.py:128
  89.2 31.4 %copy-start.21 = (pred[256,256]{0,1:T(8,128)(4,1)S(1)}, pred[256,256]{0,1:T(8,128)(4,1)}, u32[]{:S(2)}) copy-start(pred[256,256]{0,1:T(8,128)(4,1)} %and_and_fusion.4) | copy-start | bytes 196612
  90.9 27.8 %collective-permute-start.1 = (bf16[256,2,256]{0,2,1:T(8,128)(2,1)}, bf16[256,2,256]{0,2,1:T(8,128)(2,1)S(1)}, u32[]{:S(2)}, u32[]{:S(2)}) collective-permute-start(bf16[256,2,256]{0,2,1:T(8,128)(2,1)} %collective-permute-done), channel_id=1, source_target_pairs={{0,8},{8,16},{16,24},{24,32},{32,40},{40,48},{48,56},{56,64},{64,7... | collective-permute-start | bytes 786440 | tf_op jit(solution)/shard_map/ppermute | solution.py:16
  95.3 71.0 %copy-start.5 = (bf16[256,1,256]{0,2,1:T(8,128)(2,1)}, bf16[256,1,256]{0,2,1:T(8,128)(2,1)S(1)}, u32[]{:S(2)}) copy-start(bf16[256,1,256]{0,2,1:T(8,128)(2,1)S(1)} %get-tuple-element.38) | copy-start | bytes 393220
  95.3 36.9 %copy-start.19 = (pred[256,256]{0,1:T(8,128)(4,1)S(1)}, pred[256,256]{0,1:T(8,128)(4,1)}, u32[]{:S(2)}) copy-start(pred[256,256]{0,1:T(8,128)(4,1)} %get-tuple-element.44) | copy-start | bytes 196612
  118.7 11.6 %collective-permute-start.2 = (bf16[256,2,256]{0,2,1:T(8,128)(2,1)S(1)}, bf16[256,2,256]{0,2,1:T(8,128)(2,1)S(1)}, u32[]{:S(2)}, u32[]{:S(2)}) collective-permute-start(bf16[256,2,256]{0,2,1:T(8,128)(2,1)S(1)} %collective-permute-done.1), channel_id=1, source_target_pairs={{0,8},{8,16},{16,24},{24,32},{32,40},{40,48},{48,56},{56,64},{64,7... | collective-permute-start | bytes 786440 | tf_op jit(solution)/shard_map/ppermute | solution.py:16
  120.6 45.9 %copy-start.7 = (bf16[256,1,256]{0,2,1:T(8,128)(2,1)}, bf16[256,1,256]{0,2,1:T(8,128)(2,1)S(1)}, u32[]{:S(2)}) copy-start(bf16[256,1,256]{0,2,1:T(8,128)(2,1)S(1)} %get-tuple-element.36) | copy-start | bytes 393220
  120.7 22.9 %copy-start.18 = (pred[256,256]{0,1:T(8,128)(4,1)S(1)}, pred[256,256]{0,1:T(8,128)(4,1)}, u32[]{:S(2)}) copy-start(pred[256,256]{0,1:T(8,128)(4,1)} %get-tuple-element.41) | copy-start | bytes 196612
  130.3 11.3 %collective-permute-start.3 = (bf16[256,2,256]{0,2,1:T(8,128)(2,1)S(1)}, bf16[256,2,256]{0,2,1:T(8,128)(2,1)S(1)}, u32[]{:S(2)}, u32[]{:S(2)}) collective-permute-start(bf16[256,2,256]{0,2,1:T(8,128)(2,1)S(1)} %collective-permute-done.2), channel_id=1, source_target_pairs={{0,8},{8,16},{16,24},{24,32},{32,40},{40,48},{48,56},{56,64},{64,7... | collective-permute-start | bytes 786440 | tf_op jit(solution)/shard_map/ppermute | solution.py:16
  132.2 34.6 %copy-start.9 = (bf16[256,1,256]{0,2,1:T(8,128)(2,1)}, bf16[256,1,256]{0,2,1:T(8,128)(2,1)S(1)}, u32[]{:S(2)}) copy-start(bf16[256,1,256]{0,2,1:T(8,128)(2,1)S(1)} %get-tuple-element.34) | copy-start | bytes 393220
  132.3 22.7 %copy-start.17 = (pred[256,256]{0,1:T(8,128)(4,1)S(1)}, pred[256,256]{0,1:T(8,128)(4,1)}, u32[]{:S(2)}) copy-start(pred[256,256]{0,1:T(8,128)(4,1)} %get-tuple-element.42) | copy-start | bytes 196612
  141.6 11.3 %collective-permute-start.4 = (bf16[256,2,256]{0,2,1:T(8,128)(2,1)S(1)}, bf16[256,2,256]{0,2,1:T(8,128)(2,1)S(1)}, u32[]{:S(2)}, u32[]{:S(2)}) collective-permute-start(bf16[256,2,256]{0,2,1:T(8,128)(2,1)S(1)} %collective-permute-done.3), channel_id=1, source_target_pairs={{0,8},{8,16},{16,24},{24,32},{32,40},{40,48},{48,56},{56,64},{64,7... | collective-permute-start | bytes 786440 | tf_op jit(solution)/shard_map/ppermute | solution.py:16
  143.5 24.1 %copy-start.11 = (bf16[256,1,256]{0,2,1:T(8,128)(2,1)}, bf16[256,1,256]{0,2,1:T(8,128)(2,1)S(1)}, u32[]{:S(2)}) copy-start(bf16[256,1,256]{0,2,1:T(8,128)(2,1)S(1)} %get-tuple-element.32) | copy-start | bytes 393220
  143.5 20.6 %copy-start.16 = (pred[256,256]{0,1:T(8,128)(4,1)S(1)}, pred[256,256]{0,1:T(8,128)(4,1)}, u32[]{:S(2)}) copy-start(pred[256,256]{0,1:T(8,128)(4,1)} %get-tuple-element.43) | copy-start | bytes 196612
  152.8 11.3 %collective-permute-start.5 = (bf16[256,2,256]{0,2,1:T(8,128)(2,1)S(1)}, bf16[256,2,256]{0,2,1:T(8,128)(2,1)S(1)}, u32[]{:S(2)}, u32[]{:S(2)}) collective-permute-start(bf16[256,2,256]{0,2,1:T(8,128)(2,1)S(1)} %collective-permute-done.4), channel_id=1, source_target_pairs={{0,8},{8,16},{16,24},{24,32},{32,40},{40,48},{48,56},{56,64},{64,7... | collective-permute-start | bytes 786440 | tf_op jit(solution)/shard_map/ppermute | solution.py:16
  154.9 12.9 %copy-start.13 = (bf16[256,1,256]{0,2,1:T(8,128)(2,1)}, bf16[256,1,256]{0,2,1:T(8,128)(2,1)S(1)}, u32[]{:S(2)}) copy-start(bf16[256,1,256]{0,2,1:T(8,128)(2,1)S(1)} %get-tuple-element.30) | copy-start | bytes 393220
  (17 other events, 51.7 us)
